TPU v7x, 256 devices: a whole 4x4x8 slice. The times are simulated.
256 devices in a mesh: seq: 16 (over x, z_lo, core), hid: 16 (over z_hi, y).
Axes of the slice: x: 4, y: 4, z: 8 (z_hi: 4, z_lo: 2; z = z_hi * 2 + z_lo), core: 2. Of those that a mesh axis runs over, the one named last changes fastest.
Arguments:
- stream: bfloat16 [8192, 2048], P('seq'), may hold values from -5 to 5
- queries: bfloat16 [8192, 16, 128], P('seq', 'hid'), may hold values from -150 to 150
- key_rows: bfloat16 [8192, 16, 128], P('seq', 'hid'), may hold values from -5 to 5
- value_rows: bfloat16 [8192, 16, 128], P('seq', 'hid'), may hold values from -5 to 5
- segment_ids: int32 [8192], replicated, may hold values from 0 to 3, never falling along the last dimension, each value on 1 to 4096 neighbouring positions
- out_proj: bfloat16 [16, 128, 2048], P('hid'), may hold values from -0.125 to 0.125
- norm_gain: float32 [2048], replicated, may hold values from 0.1 to 1.9
- expert_ids: int32 [8192, 6], P('seq'), may hold values from 0 to 63, all different within a row; in each aligned block of 512 rows (0 to 511, 512 to 1023, ...) at most 64 rows name the same one
- route_gates: float32 [8192, 6], P('seq'), may hold values from 0.05 to 0.4
- gate_proj: bfloat16 [90112, 2048], P(('seq', 'hid')), may hold values from -0.125 to 0.125
- up_proj: bfloat16 [90112, 2048], P(('seq', 'hid')), may hold values from -0.125 to 0.125
- down_proj: bfloat16 [90112, 2048], P(('seq', 'hid')), may hold values from -0.15625 to 0.15625
- shared_gate: bfloat16 [2816, 2048], P('hid'), may hold values from -0.125 to 0.125
- shared_up: bfloat16 [2816, 2048], P('hid'), may hold values from -0.125 to 0.125
- shared_down: bfloat16 [2816, 2048], P('hid'), may hold values from -0.109375 to 0.109375
Outputs:
- layer_out: bfloat16 [8192, 2048], P('seq', 'hid')
Inputs may be any that keep to these rules, and one draw needn't show every extreme that they name: `segment_ids`: segment numbers never fall along the tokens; every segment has at most 4096 tokens and one has exactly 4096. `expert_ids`: the 6 experts of a token differ; among the 512 tokens of one index of seq no expert is named by more than 64 tokens, a bound that some block reaches of them.
All inputs are finite; a program needn't handle non-finite values.
Results may differ from a plain program's by a relative error of at most 0.019.
Values may be sent and summed in bfloat16 or wider, within the bound.
No kernel may reach another device: no remote copies, remote signals or barrier semaphores. Data moves between devices by JAX's collectives and lax.ppermute only.
A program may use at most 128 MiB of HBM per device.

v0:
```python
import jax
import jax.numpy as jnp
from jax import lax
from jax.sharding import PartitionSpec as P

EXPERTS = 64
FF = 1408
TOP = 6
CAP = 64


def on_device(
    stream,
    queries,
    key_rows,
    value_rows,
    segment_ids,
    out_proj,
    norm_gain,
    expert_ids,
    route_gates,
    gate_proj,
    up_proj,
    down_proj,
    shared_gate,
    shared_up,
    shared_down,
):
    tok_count = queries.shape[0]
    local_heads = queries.shape[1]
    head_width = queries.shape[2]
    width = stream.shape[1]
    inv_root = head_width ** (-0.5)
    seq_count = lax.axis_size("seq")
    hid_count = lax.axis_size("hid")
    hid_index = lax.axis_index("hid")
    query_first = lax.axis_index("seq") * tok_count
    query_seg = lax.dynamic_slice_in_dim(segment_ids, query_first, tok_count)
    query_pos = query_first + jnp.arange(tok_count, dtype=jnp.int32)
    run_max = jnp.full((tok_count, local_heads), -1e30, jnp.float32)
    key_part = lax.all_gather(key_rows, "seq", axis=0, tiled=True)
    value_part = lax.all_gather(value_rows, "seq", axis=0, tiled=True)
    row_count = key_part.shape[0]
    key_pos = jnp.arange(row_count, dtype=jnp.int32)
    scores = (
        jnp.einsum("qhd,khd->qhk", queries, key_part, preferred_element_type=jnp.float32) * inv_root
    )
    allowed = (query_seg[:, None] == segment_ids[None, :]) & (
        key_pos[None, :] <= query_pos[:, None]
    )
    scores = jnp.where(allowed[:, None, :], scores, -1e30)
    new_max = jnp.maximum(run_max, jnp.max(scores, axis=2))
    weights = jnp.where(allowed[:, None, :], jnp.exp(scores - new_max[:, :, None]), 0.0)
    new_sum = jnp.sum(weights, axis=2)
    probs = weights.astype(jnp.bfloat16)
    new_acc = jnp.einsum("qhk,khd->qhd", probs, value_part, preferred_element_type=jnp.float32)
    attended = (
        (new_acc / new_sum[:, :, None])
        .astype(jnp.bfloat16)
        .reshape(tok_count, local_heads * head_width)
    )
    out_flat = out_proj.reshape(local_heads * head_width, width)
    partial_mix = jnp.dot(attended, out_flat, preferred_element_type=jnp.float32)
    mixed = stream.astype(jnp.float32) + lax.psum(partial_mix.astype(jnp.bfloat16), "hid").astype(
        jnp.float32
    )
    mean_square = jnp.mean(mixed * mixed, axis=1, keepdims=True)
    normed = (mixed * lax.rsqrt(mean_square + 1e-06) * norm_gain).astype(jnp.bfloat16)
    shared_gate_val = jnp.einsum(
        "td,fd->tf", normed, shared_gate, preferred_element_type=jnp.float32
    )
    shared_up_val = jnp.einsum("td,fd->tf", normed, shared_up, preferred_element_type=jnp.float32)
    shared_act = (jax.nn.silu(shared_gate_val) * shared_up_val).astype(jnp.bfloat16)
    shared_part = jnp.dot(shared_act, shared_down, preferred_element_type=jnp.float32)
    shared_out = lax.psum_scatter(
        shared_part.astype(jnp.bfloat16), "hid", scatter_dimension=1, tiled=True
    ).astype(jnp.float32)
    col_count = shared_out.shape[1]
    unit_rows = gate_proj.shape[0]
    held_count = max(1, unit_rows // FF)
    held_units = unit_rows // held_count
    local_experts = EXPERTS // seq_count
    first_local = hid_index * unit_rows // FF
    flat_ids = expert_ids.reshape(-1)
    onehot = (flat_ids[:, None] == jnp.arange(EXPERTS, dtype=jnp.int32)[None, :]).astype(jnp.int32)
    slot_rank = jnp.sum((jnp.cumsum(onehot, axis=0) - 1) * onehot, axis=1)
    owner_group = flat_ids // local_experts
    local_expert = flat_ids % local_experts
    held_offset = local_expert - first_local
    is_held = (held_offset >= 0) & (held_offset < held_count)
    slot_total = seq_count * held_count * CAP
    send_index = jnp.where(
        is_held, (owner_group * held_count + held_offset) * CAP + slot_rank, slot_total
    )
    route_token = jnp.arange(tok_count * TOP, dtype=jnp.int32) // TOP
    slot_token = jnp.full((slot_total,), -1, jnp.int32).at[send_index].set(route_token, mode="drop")
    send_rows = jnp.where(
        (slot_token >= 0)[:, None], normed[jnp.maximum(slot_token, 0)], jnp.zeros((), jnp.bfloat16)
    )
    send_rows = send_rows.reshape(seq_count, held_count, CAP, width)
    received = lax.all_to_all(send_rows, "seq", split_axis=0, concat_axis=0, tiled=True)
    gate_local = gate_proj.reshape(held_count, held_units, width)
    up_local = up_proj.reshape(held_count, held_units, width)
    down_local = down_proj.reshape(held_count, held_units, hid_count, col_count)
    gate_val = jnp.einsum(
        "sicd,ifd->sicf", received, gate_local, preferred_element_type=jnp.float32
    )
    up_val = jnp.einsum("sicd,ifd->sicf", received, up_local, preferred_element_type=jnp.float32)
    expert_act = (jax.nn.silu(gate_val) * up_val).astype(jnp.bfloat16)
    down_part = jnp.einsum(
        "sicf,ifnx->niscx", expert_act, down_local, preferred_element_type=jnp.float32
    ).astype(jnp.bfloat16)
    down_part = down_part.reshape(hid_count, held_count, seq_count * CAP, col_count)
    peer_parts = lax.all_to_all(down_part, "hid", split_axis=0, concat_axis=0, tiled=True)
    part_count = hid_count * held_count // local_experts
    expert_out = jnp.sum(
        peer_parts.reshape(local_experts, part_count, seq_count * CAP, col_count).astype(
            jnp.float32
        ),
        axis=1,
    ).astype(jnp.bfloat16)
    returned = lax.all_to_all(
        expert_out.reshape(local_experts, seq_count, CAP, col_count),
        "seq",
        split_axis=1,
        concat_axis=1,
        tiled=True,
    ).reshape(-1, col_count)
    pick_index = local_expert * (seq_count * CAP) + owner_group * CAP + slot_rank
    picked = returned[pick_index].reshape(tok_count, TOP, col_count)
    routed_sum = jnp.einsum("tj,tjd->td", route_gates, picked.astype(jnp.float32))
    mixed_cols = lax.dynamic_slice_in_dim(mixed, hid_index * col_count, col_count, 1)
    return (mixed_cols + shared_out + routed_sum).astype(jnp.bfloat16)


def solution(mesh):
    placed = (
        P("seq", None),
        P("seq", "hid", None),
        P("seq", "hid", None),
        P("seq", "hid", None),
        P(),
        P("hid", None, None),
        P(),
        P("seq", None),
        P("seq", None),
        P(("seq", "hid"), None),
        P(("seq", "hid"), None),
        P(("seq", "hid"), None),
        P("hid", None),
        P("hid", None),
        P("hid", None),
    )
    return jax.shard_map(
        on_device, mesh=mesh, in_specs=placed, out_specs=P("seq", "hid"), check_vma=False
    )
```

profile of v0, /device:TPU:2, one launch (start us, length us, event | category | flops | bytes accessed | tf_op | source)
XLA Modules:
  0.0 560.0 jit_solution(7915488398288904833)
XLA Ops:
  9.7 18.3 %reduce-window.6 = s32[64,24,128]{2,1,0:T(8,128)S(1)} reduce-window(s32[64,24,128]{2,1,0:T(8,128)S(1)} %fusion.60, s32[]{:T(128)} %constant.78.clone.1), window={size=1x1x128 pad=0_0x0_0x127_0}, to_apply=%region_5.6 | reduce-window | flops 24969216 | bytes 1572868 | tf_op jit(solution)/shard_map/reduce-window
  29.6 18.4 %all-gather.3.cloned.1.call-done = bf16[8192,1,128]{2,0,1:T(8,128)(2,1)} async-done(((bf16[512,1,128]{2,0,1:T(8,128)(2,1)}), bf16[8192,1,128]{2,0,1:T(8,128)(2,1)}) %all-gather.3.cloned.1.call-update) | async-done | bytes 2097168 | tf_op jit(solution)/shard_map/all_gather | solution.py:41
  48.1 7.0 %fusion.1 = (f32[512]{0:T(512)S(1)}, f32[8192,512]{1,0:T(8,128)S(1)}) fusion(s32[512]{0:T(512)S(1)} %iota_add_fusion, s32[512]{0:T(512)S(1)} %dynamic_slice.6, s32[8192]{0:T(1024)S(1)} %copy-done.10, bf16[512,1,128]{2,0,1:T(8,128)(2,1)S(1)} %copy-done.16, bf16[8192,1,128]{2,0,1:T(8,128)(2,1)} %all-gather.3.cloned.1.call-done), kind=kOutput, calls=%fused_computation.7 | convolution fusion | flops 1098907136 | bytes 19044352 | tf_op jit(solution)/shard_map/qhd,khd->qhk/dot_general | solution.py:46
  55.1 5.7 %copy-done.1 = f32[8192,512]{1,0:T(8,128)} copy-done((f32[8192,512]{1,0:T(8,128)}, f32[8192,512]{1,0:T(8,128)S(1)}, u32[]{:S(2)}) %copy-start.1) | copy-done | bytes 16777240
  60.8 5.8 %fusion.2 = f32[512]{0:T(512)S(1)} fusion(f32[8192,512]{1,0:T(8,128)S(1)} %get-tuple-element.11, f32[512]{0:T(512)S(1)} %broadcast_maximum_fusion, s32[512]{0:T(512)S(1)} %iota_add_fusion, s32[512]{0:T(512)S(1)} %dynamic_slice.6, s32[8192]{0:T(1024)S(1)} %copy-done.10), kind=kLoop, calls=%fused_computation.8 | loop fusion | flops 33553920 | bytes 16818176 | tf_op jit(solution)/shard_map/reduce_sum | solution.py:54
  66.6 19.7 %all-gather.5.cloned.1.call-done = bf16[8192,1,128]{2,0,1:T(8,128)(2,1)} async-done(((bf16[512,1,128]{2,0,1:T(8,128)(2,1)}), bf16[8192,1,128]{2,0,1:T(8,128)(2,1)}) %all-gather.5.cloned.1.call-update) | async-done | bytes 2097168 | tf_op jit(solution)/shard_map/all_gather | solution.py:42
  86.3 14.9 %convolution_convert_fusion.1 = bf16[512,2048]{1,0:T(8,128)(2,1)} fusion(bf16[8192,1,128]{2,0,1:T(8,128)(2,1)} %all-gather.5.cloned.1.call-done, f32[8192,512]{1,0:T(8,128)} %copy-done.1, f32[512]{0:T(512)S(1)} %broadcast_maximum_fusion, s32[512]{0:T(512)S(1)} %iota_add_fusion, s32[512]{0:T(512)S(1)} %dynamic_slice.6, s32[8192]{0:T(1024)S(1)} %copy-done.10, ...), kind=kOutput, calls=%fused_computation.23 | convolution fusion | flops 1376911360 | bytes 21536768 | tf_op jit(solution)/shard_map/dot_general | solution.py:63
  109.2 12.1 %scatter_custom_fusion = s32[1024]{0:T(1024)S(1)} fusion(s32[3072]{0:T(1024)S(1)} %bitcast.215, s32[3072]{0:T(1024)} %add_select_fusion, s32[]{:T(128)} %constant.89.clone.1), kind=kCustom, calls=%fused_computation.81 | custom fusion | bytes 4608 | tf_op jit(solution)/shard_map/scatter | solution.py:96
  122.0 158.6 %all-reduce.2.cloned.1.call-done = bf16[512,2048]{1,0:T(8,128)(2,1)} async-done(((bf16[512,2048]{1,0:T(8,128)(2,1)}), bf16[512,2048]{1,0:T(8,128)(2,1)}) %all-reduce.2.cloned.1.call-update) | async-done | bytes 2097168 | tf_op jit(solution)/shard_map/psum | solution.py:64
  280.6 4.3 convert_add_fusion
  286.2 6.1 %gather_fusion = bf16[1024,2048]{1,0:T(8,128)(2,1)} fusion(bf16[512,2048]{1,0:T(8,128)(2,1)S(1)} %multiply_convert_fusion, s32[1024]{0:T(1024)S(1)} %maximum_clamp_fusion), kind=kCustom, calls=%fused_computation | custom fusion | bytes 8392704 | tf_op jit(solution)/shard_map/gather | solution.py:98
  294.8 52.4 %all_to_all.15 = bf16[16,1,64,2048]{3,2,1,0:T(8,128)(2,1)S(1)} all-to-all(bf16[16,1,64,2048]{3,2,1,0:T(8,128)(2,1)S(1)} %broadcast_select_fusion), channel_id=1, replica_groups=mesh['seq'=16,'hid'=16] {'seq'}, dimensions={0} | all-to-all | bytes 8388608 | tf_op jit(solution)/shard_map/all_to_all | solution.py:101
  349.2 3.5 fusion.9
  352.7 8.3 %convert_bitcast_fusion = bf16[16,1,16,64,128]{4,3,0,2,1:T(8,128)(2,1)} fusion(bf16[352,2048]{1,0:T(8,128)(2,1)S(1)} %copy-done, bf16[16,1,64,2048]{3,2,1,0:T(8,128)(2,1)} %copy-done.6, f32[16,64,352]{2,1,0:T(8,128)} %fusion.9, bf16[352,2048]{1,0:T(8,128)(2,1)} %param.26), kind=kOutput, calls=%fused_computation.17 | convolution fusion | flops 2957049856 | bytes 12713984 | tf_op jit(solution)/shard_map/sicf,ifnx->niscx/dot_general | solution.py:110
  361.0 5.6 copy.41
  366.6 6.0 %all-to-all-start.1 = ((bf16[16,1,1024,128]{3,2,1,0:T(8,128)(2,1)}), bf16[16,1,1024,128]{3,2,1,0:T(8,128)(2,1)}, u32[]{:S(2)}, u32[]{:S(2)}) async-start(bf16[16,1,1024,128]{3,2,1,0:T(8,128)(2,1)} %bitcast.203), calls=%async_computation.1 | async-start | bytes 8388608 | tf_op jit(solution)/shard_map/all_to_all | solution.py:114
  372.6 2.7 fusion.83
  375.3 4.3 convolution_convert_fusion
  379.7 3.9 copy.49
  383.6 82.5 %all-to-all-done.1 = bf16[16,1,1024,128]{3,2,1,0:T(8,128)(2,1)} async-done(((bf16[16,1,1024,128]{3,2,1,0:T(8,128)(2,1)}), bf16[16,1,1024,128]{3,2,1,0:T(8,128)(2,1)}, u32[]{:S(2)}, u32[]{:S(2)}) %all-to-all-start.1) | async-done | bytes 4194336 | tf_op jit(solution)/shard_map/all_to_all | solution.py:114
  466.1 2.9 bitcast_reduce_fusion
  470.0 29.8 %all-to-all-start.2 = ((bf16[4,16,64,128]{3,2,0,1:T(8,128)(2,1)}), bf16[4,16,64,128]{3,2,0,1:T(8,128)(2,1)S(1)}, u32[]{:S(2)}, u32[]{:S(2)}) async-start(bf16[4,16,64,128]{3,2,0,1:T(8,128)(2,1)} %copy.43), calls=%async_computation.2 | async-start | bytes 2097152 | tf_op jit(solution)/shard_map/all_to_all | solution.py:122
  500.8 38.2 %reduce-scatter.4.cloned.1.call-done = bf16[128,512]{1,0:T(8,128)(2,1)} async-done(((bf16[2048,512]{1,0:T(8,128)(2,1)}), bf16[128,512]{1,0:T(8,128)(2,1)}) %reduce-scatter.4.cloned.1.call-update) | async-done | bytes 131088
  540.7 9.2 %gather_fusion.1 = bf16[3072,128]{1,0:T(8,128)(2,1)S(1)} fusion(bf16[4096,128]{1,0:T(8,128)(2,1)S(1)} %bitcast.201, s32[3072]{0:T(1024)S(1)} %broadcast_clamp_fusion), kind=kCustom, calls=%fused_computation.1 | custom fusion | bytes 1585152 | tf_op jit(solution)/shard_map/gather | solution.py:130
  (72 shorter events, 26.4 us)
Async XLA Ops:
  6.5 346.2 %copy-start = (bf16[352,2048]{1,0:T(8,128)(2,1)S(1)}, bf16[352,2048]{1,0:T(8,128)(2,1)}, u32[]{:S(2)}) copy-start(bf16[352,2048]{1,0:T(8,128)(2,1)} %param.25) | copy-start | bytes 4325380
  6.5 23.0 %copy-start.10 = (s32[8192]{0:T(1024)S(1)}, s32[8192]{0:T(1024)}, u32[]{:S(2)}) copy-start(s32[8192]{0:T(1024)} %param.19) | copy-start | bytes 98308
  6.5 41.6 %copy-start.16 = (bf16[512,1,128]{2,0,1:T(8,128)(2,1)S(1)}, bf16[512,1,128]{2,0,1:T(8,128)(2,1)}, u32[]{:S(2)}) copy-start(bf16[512,1,128]{2,0,1:T(8,128)(2,1)} %param.16) | copy-start | bytes 393220
  6.5 41.6 %all-gather.3.cloned.1.call-start = ((), (), s32[]{:S(2)}) async-start(), calls=%async_computation.4 | async-start | bytes 2228224 | tf_op jit(solution)/shard_map/all_gather | solution.py:41
  7.3 79.0 %all-gather.5.cloned.1.call-start = ((), (), s32[]{:S(2)}) async-start(), calls=%async_computation.5 | async-start | bytes 2228224 | tf_op jit(solution)/shard_map/all_gather | solution.py:42
  8.0 272.6 %all-reduce.2.cloned.1.call-start = ((), (), s32[]{:S(2)}) async-start(), calls=%async_computation.6 | async-start | bytes 4194304 | tf_op jit(solution)/shard_map/psum | solution.py:64
  8.9 0.7 copy-start.7
  28.0 27.0 %copy-start.5 = (s32[64,24,128]{2,1,0:T(8,128)}, s32[64,24,128]{2,1,0:T(8,128)S(1)}, u32[]{:S(2)}) copy-start(s32[64,24,128]{2,1,0:T(8,128)S(1)} %reduce-window.6) | copy-start | bytes 2359300
  55.1 5.7 %copy-start.1 = (f32[8192,512]{1,0:T(8,128)}, f32[8192,512]{1,0:T(8,128)S(1)}, u32[]{:S(2)}) copy-start(f32[8192,512]{1,0:T(8,128)S(1)} %get-tuple-element.11) | copy-start | bytes 50331652
  60.8 25.5 %copy-start.15 = (bf16[1,128,2048]{2,1,0:T(8,128)(2,1)S(1)}, bf16[1,128,2048]{2,1,0:T(8,128)(2,1)}, u32[]{:S(2)}) copy-start(bf16[1,128,2048]{2,1,0:T(8,128)(2,1)} %param.20) | copy-start | bytes 1572868
  101.2 179.4 %copy-start.2 = (bf16[512,2048]{1,0:T(8,128)(2,1)S(1)}, bf16[512,2048]{1,0:T(8,128)(2,1)}, u32[]{:S(2)}) copy-start(bf16[512,2048]{1,0:T(8,128)(2,1)} %param.15) | copy-start | bytes 6291460
  122.0 163.0 %copy-start.12 = (f32[2048]{0:T(1024)S(1)}, f32[2048]{0:T(1024)}, u32[]{:S(2)}) copy-start(f32[2048]{0:T(1024)} %param.21) | copy-start | bytes 24580
  280.6 4.4 copy-start.3
  280.6 4.4 copy-start.4
  286.1 6.1 %copy-start.13 = (pred[16,64]{1,0:T(8,128)(4,1)S(1)}, pred[16,64]{1,0:T(8,128)(4,1)}, u32[]{:S(2)}) copy-start(pred[16,64]{1,0:T(8,128)(4,1)} %broadcast_in_dim.53) | copy-start | bytes 3076
  294.8 54.4 %copy-start.14 = (bf16[352,2048]{1,0:T(8,128)(2,1)S(1)}, bf16[352,2048]{1,0:T(8,128)(2,1)}, u32[]{:S(2)}) copy-start(bf16[352,2048]{1,0:T(8,128)(2,1)} %param.24) | copy-start | bytes 4325380
  347.2 2.0 copy-start.6
  366.6 99.5 %all-to-all-start.1 = ((bf16[16,1,1024,128]{3,2,1,0:T(8,128)(2,1)}), bf16[16,1,1024,128]{3,2,1,0:T(8,128)(2,1)}, u32[]{:S(2)}, u32[]{:S(2)}) async-start(bf16[16,1,1024,128]{3,2,1,0:T(8,128)(2,1)} %bitcast.203), calls=%async_computation.1 | async-start | bytes 8388608 | tf_op jit(solution)/shard_map/all_to_all | solution.py:114
  372.6 166.4 %reduce-scatter.4.cloned.1.call-start = ((), (), s32[]{:S(2)}) async-start(), calls=%async_computation.7 | async-start | bytes 2228224
  466.1 33.8 %copy-start.11 = (f32[512,6]{0,1:T(8,128)S(1)}, f32[512,6]{0,1:T(8,128)}, u32[]{:S(2)}) copy-start(f32[512,6]{0,1:T(8,128)} %param.23) | copy-start | bytes 36868
  466.1 34.7 %copy-start.9 = (s32[3072,1]{0,1:T(1,128)S(1)}, s32[3072,1]{0,1:T(1,128)}, u32[]{:S(2)}) copy-start(s32[3072,1]{0,1:T(1,128)} %get-tuple-element.5) | copy-start | bytes 36868
  470.0 70.6 %all-to-all-start.2 = ((bf16[4,16,64,128]{3,2,0,1:T(8,128)(2,1)}), bf16[4,16,64,128]{3,2,0,1:T(8,128)(2,1)S(1)}, u32[]{:S(2)}, u32[]{:S(2)}) async-start(bf16[4,16,64,128]{3,2,0,1:T(8,128)(2,1)} %copy.43), calls=%async_computation.2 | async-start | bytes 2097152 | tf_op jit(solution)/shard_map/all_to_all | solution.py:122
  540.7 11.1 %copy-start.8 = (bf16[512,128]{1,0:T(8,128)(2,1)S(1)}, bf16[512,128]{1,0:T(8,128)(2,1)}, u32[]{:S(2)}) copy-start(bf16[512,128]{1,0:T(8,128)(2,1)} %copy.50) | copy-start | bytes 393220
Sparse Core Ops, SparseCore 0:
  9.2 38.8 all-gather.2
  49.9 36.3 all-gather.4
  101.3 179.2 all-reduce.1
  383.7 155.2 reduce-scatter.3
where the time goes:
time: 561 us; the launch traced here: 560 us
  waiting for transfers between devices  319 us (57%)
  local copies, waits for them, and re-layouts  54.4 us (10%)
  blocking collectives  52.4 us (9%)
  other arithmetic  42.7 us (8%)
  matrix products  42.4 us (8%)
  starting transfers between devices  35.9 us (6%)
  between operations  13.4 us (2%)
    psum x1, waiting for transfers between devices, on_device(): lax.psum(partial_mix.astype(jnp.bfloat16), 'hid').astype(jnp.float32)  159 us
    all_to_all x1, waiting for transfers between devices, on_device(): lax.all_to_all(down_part, 'hid', split_axis=0, concat_axis=0, tiled=True)  82.5 us
    all_to_all x1, blocking collectives, on_device(): lax.all_to_all(send_rows, 'seq', split_axis=0, concat_axis=0, tiled=True)  52.4 us
    unnamed x5, waiting for transfers between devices  39.6 us
    all_to_all x1, starting transfers between devices, on_device(): lax.all_to_all(expert_out.reshape(local_experts, seq_count, CAP, col_coun...  29.8 us
    all_gather x1, waiting for transfers between devices, on_device(): value_part = lax.all_gather(value_rows, 'seq', axis=0, tiled=True)  19.7 us
    another operation x2, other arithmetic  19.2 us
    all_gather x1, waiting for transfers between devices, on_device(): key_part = lax.all_gather(key_rows, 'seq', axis=0, tiled=True)  18.4 us
  transfers between devices with their start and end apart: 6, of which 5 were waited for; matrix products, arithmetic and copies ran while one was open for 13% of the time, Pallas kernels for 0%

commit v1 on v0

--- a/solution.py
+++ b/solution.py
@@ -7,6 +7,24 @@
 FF = 1408
 TOP = 6
 CAP = 64
+
+
+def seq_gather(rows, seq_count):
+    spread = jnp.broadcast_to(rows[None], (seq_count,) + rows.shape)
+    got = lax.all_to_all(spread, "seq", split_axis=0, concat_axis=0, tiled=True)
+    return got.reshape((seq_count * rows.shape[0],) + rows.shape[1:])
+
+
+def hid_scatter_sum(part, hid_count):
+    rows, width = part.shape
+    got = lax.all_to_all(
+        part.reshape(rows, hid_count, width // hid_count),
+        "hid",
+        split_axis=1,
+        concat_axis=1,
+        tiled=True,
+    )
+    return jnp.sum(got.astype(jnp.float32), axis=1)
 
 
 def on_device(
@@ -38,8 +56,8 @@
     query_seg = lax.dynamic_slice_in_dim(segment_ids, query_first, tok_count)
     query_pos = query_first + jnp.arange(tok_count, dtype=jnp.int32)
     run_max = jnp.full((tok_count, local_heads), -1e30, jnp.float32)
-    key_part = lax.all_gather(key_rows, "seq", axis=0, tiled=True)
-    value_part = lax.all_gather(value_rows, "seq", axis=0, tiled=True)
+    key_part = seq_gather(key_rows, seq_count)
+    value_part = seq_gather(value_rows, seq_count)
     row_count = key_part.shape[0]
     key_pos = jnp.arange(row_count, dtype=jnp.int32)
     scores = (
@@ -61,21 +79,36 @@
     )
     out_flat = out_proj.reshape(local_heads * head_width, width)
     partial_mix = jnp.dot(attended, out_flat, preferred_element_type=jnp.float32)
-    mixed = stream.astype(jnp.float32) + lax.psum(partial_mix.astype(jnp.bfloat16), "hid").astype(
+    col_count = width // hid_count
+    col_first = hid_index * col_count
+    mixed_cols = lax.dynamic_slice_in_dim(stream, col_first, col_count, 1).astype(
         jnp.float32
+    ) + hid_scatter_sum(partial_mix.astype(jnp.bfloat16), hid_count)
+    square_part = jnp.sum(mixed_cols * mixed_cols, axis=1)
+    square_all = lax.all_to_all(
+        jnp.broadcast_to(square_part[None, :], (hid_count, tok_count)),
+        "hid",
+        split_axis=0,
+        concat_axis=0,
+        tiled=True,
     )
-    mean_square = jnp.mean(mixed * mixed, axis=1, keepdims=True)
-    normed = (mixed * lax.rsqrt(mean_square + 1e-06) * norm_gain).astype(jnp.bfloat16)
+    mean_square = (jnp.sum(square_all, axis=0) / width)[:, None]
+    gain_cols = lax.dynamic_slice_in_dim(norm_gain, col_first, col_count, 0)
+    normed_cols = (mixed_cols * lax.rsqrt(mean_square + 1e-06) * gain_cols).astype(jnp.bfloat16)
+    normed = lax.all_to_all(
+        jnp.broadcast_to(normed_cols[:, None, :], (tok_count, hid_count, col_count)),
+        "hid",
+        split_axis=1,
+        concat_axis=1,
+        tiled=True,
+    ).reshape(tok_count, width)
     shared_gate_val = jnp.einsum(
         "td,fd->tf", normed, shared_gate, preferred_element_type=jnp.float32
     )
     shared_up_val = jnp.einsum("td,fd->tf", normed, shared_up, preferred_element_type=jnp.float32)
     shared_act = (jax.nn.silu(shared_gate_val) * shared_up_val).astype(jnp.bfloat16)
     shared_part = jnp.dot(shared_act, shared_down, preferred_element_type=jnp.float32)
-    shared_out = lax.psum_scatter(
-        shared_part.astype(jnp.bfloat16), "hid", scatter_dimension=1, tiled=True
-    ).astype(jnp.float32)
-    col_count = shared_out.shape[1]
+    shared_out = hid_scatter_sum(shared_part.astype(jnp.bfloat16), hid_count)
     unit_rows = gate_proj.shape[0]
     held_count = max(1, unit_rows // FF)
     held_units = unit_rows // held_count
@@ -129,7 +162,6 @@
     pick_index = local_expert * (seq_count * CAP) + owner_group * CAP + slot_rank
     picked = returned[pick_index].reshape(tok_count, TOP, col_count)
     routed_sum = jnp.einsum("tj,tjd->td", route_gates, picked.astype(jnp.float32))
-    mixed_cols = lax.dynamic_slice_in_dim(mixed, hid_index * col_count, col_count, 1)
     return (mixed_cols + shared_out + routed_sum).astype(jnp.bfloat16)
 
 

time: 561 us -> 505 us (0.900)
  waiting for transfers between devices: 319 us -> 214 us
  blocking collectives: 52.4 us -> 82 us
  starting transfers between devices: 35.9 us -> 65.3 us
  between operations: 13.4 us -> 0.31 us
  local copies, waits for them, and re-layouts: 54.4 us -> 61.5 us
  other arithmetic: 42.7 us -> 36.3 us
    psum x1 -> x0, waiting for transfers between devices: 159 us -> none  [on_device(): lax.psum(partial_mix.astype(jnp.bfloat16), 'hid').astype(jnp.float32)]
    all_to_all x0 -> x5, waiting for transfers between devices: none -> 124 us  [the longest x2 89.7 us: hid_scatter_sum(): lax.all_to_all(part.reshape(rows, hid_count, width // hid_count), 'hid',...]
    unnamed x5 -> x0, waiting for transfers between devices: 39.6 us -> none
    all_gather x2 -> x0, waiting for transfers between devices: 38.1 us -> none  [the longest x1 19.7 us: on_device(): value_part = lax.all_gather(value_rows, 'seq', axis=0, tiled=True)]
    all_to_all x0 -> x5, starting transfers between devices: none -> 37.5 us  [the longest x2 22.8 us: hid_scatter_sum(): lax.all_to_all(part.reshape(rows, hid_count, width // hid_count), 'hid',...]
    all_to_all x0 -> x1, blocking collectives: none -> 31.2 us  [seq_gather(): got = lax.all_to_all(spread, 'seq', split_axis=0, concat_axis=0, tiled=True)]
    all_to_all x1, waiting for transfers between devices: 0.01 us -> 10.7 us  [on_device(): lax.all_to_all(expert_out.reshape(local_experts, seq_count, CAP, col_coun...]
    reshape x0 -> x3, local copies, waits for them, and re-layouts: none -> 7.31 us  [the longest x2 5.42 us: hid_scatter_sum(): part.reshape(rows, hid_count, width // hid_count)]
  transfers between devices with their start and end apart: 6 -> 7, of which waited for: 5 -> 7; matrix products, arithmetic and copies ran while one was open for 13% -> 13% of each run, Pallas kernels for 0% -> 0%
where the time goes in v1:
time: 505 us; the launch traced here: 501 us
  waiting for transfers between devices  214 us (42%)
  blocking collectives  82 us (16%)
  starting transfers between devices  65.3 us (13%)
  local copies, waits for them, and re-layouts  61.5 us (12%)
  matrix products  41.3 us (8%)
  other arithmetic  36.3 us (7%)
    all_to_all x2, waiting for transfers between devices, hid_scatter_sum(): lax.all_to_all(part.reshape(rows, hid_count, width // hid_count), 'hid',...  89.7 us
    all_to_all x1, waiting for transfers between devices, on_device(): lax.all_to_all(down_part, 'hid', split_axis=0, concat_axis=0, tiled=True)  79.5 us
    all_to_all x1, blocking collectives, on_device(): lax.all_to_all(send_rows, 'seq', split_axis=0, concat_axis=0, tiled=True)  50.8 us
    all_to_all x1, blocking collectives, seq_gather(): got = lax.all_to_all(spread, 'seq', split_axis=0, concat_axis=0, tiled=True)  31.2 us
    all_to_all x1, starting transfers between devices, on_device(): lax.all_to_all(expert_out.reshape(local_experts, seq_count, CAP, col_coun...  23.1 us
    all_to_all x2, starting transfers between devices, hid_scatter_sum(): lax.all_to_all(part.reshape(rows, hid_count, width // hid_count), 'hid',...  22.8 us
    another operation x2, other arithmetic  18.5 us
    all_to_all x1, waiting for transfers between devices, on_device(): lax.all_to_all(jnp.broadcast_to(normed_cols[:, None, :], (tok_count, hid_...  18.5 us
  transfers between devices with their start and end apart: 7, of which 7 were waited for; matrix products, arithmetic and copies ran while one was open for 13% of the time, Pallas kernels for 0%

profile of v1, /device:TPU:2, one launch (start us, length us, event | category | flops | bytes accessed | tf_op | source)
XLA Modules:
  0.0 501.3 jit_solution(10754472735202141509)
XLA Ops:
  1.4 31.2 %all_to_all.46 = bf16[16,512,1,128]{3,1,2,0:T(8,128)(2,1)} all-to-all(bf16[16,512,1,128]{3,1,2,0:T(8,128)(2,1)S(1)} %broadcast_in_dim.44), channel_id=1, replica_groups=mesh['seq'=16,'hid'=16] {'seq'}, dimensions={0} | all-to-all | bytes 4194304 | tf_op jit(solution)/shard_map/all_to_all | solution.py:14
  34.4 6.2 %all-to-all-start.1 = ((bf16[16,512,1,128]{3,1,2,0:T(8,128)(2,1)}), bf16[16,512,1,128]{3,1,2,0:T(8,128)(2,1)S(1)}, u32[]{:S(2)}, u32[]{:S(2)}) async-start(bf16[16,512,1,128]{3,1,2,0:T(8,128)(2,1)} %broadcast_in_dim.82), calls=%async_computation.1 | async-start | bytes 4194304 | tf_op jit(solution)/shard_map/all_to_all | solution.py:14
  41.4 7.1 %fusion.1 = (f32[512]{0:T(512)S(1)}, f32[8192,512]{1,0:T(8,128)S(1)}) fusion(s32[512]{0:T(512)S(1)} %iota_add_fusion, s32[512]{0:T(512)S(1)} %dynamic_slice.10, s32[8192]{0:T(1024)} %param.19, bf16[8192,128]{1,0:T(8,128)(2,1)} %bitcast.218, bf16[512,1,128]{2,0,1:T(8,128)(2,1)} %param.16), kind=kOutput, calls=%fused_computation.7 | convolution fusion | flops 1098907136 | bytes 19044352 | tf_op jit(solution)/shard_map/qhd,khd->qhk/dot_general | solution.py:64
  48.4 5.7 %copy-done.1 = f32[8192,512]{1,0:T(8,128)} copy-done((f32[8192,512]{1,0:T(8,128)}, f32[8192,512]{1,0:T(8,128)S(1)}, u32[]{:S(2)}) %copy-start.1) | copy-done | bytes 16777240
  54.1 5.8 %fusion.2 = f32[512]{0:T(512)S(1)} fusion(f32[8192,512]{1,0:T(8,128)S(1)} %get-tuple-element.9, f32[512]{0:T(512)S(1)} %broadcast_maximum_fusion, s32[512]{0:T(512)S(1)} %iota_add_fusion, s32[512]{0:T(512)S(1)} %dynamic_slice.10, s32[8192]{0:T(1024)S(1)} %copy-done.7), kind=kLoop, calls=%fused_computation.8 | loop fusion | flops 33553920 | bytes 16818176 | tf_op jit(solution)/shard_map/reduce_sum | solution.py:72
  60.0 6.8 %all-to-all-done.1 = bf16[16,512,1,128]{3,1,2,0:T(8,128)(2,1)S(1)} async-done(((bf16[16,512,1,128]{3,1,2,0:T(8,128)(2,1)}), bf16[16,512,1,128]{3,1,2,0:T(8,128)(2,1)S(1)}, u32[]{:S(2)}, u32[]{:S(2)}) %all-to-all-start.1) | async-done | bytes 2097184 | tf_op jit(solution)/shard_map/all_to_all | solution.py:14
  66.8 14.4 %fusion.11 = bf16[64,16,8,128]{3,2,1,0:T(8,128)(2,1)} fusion(bf16[8192,128]{1,0:T(8,128)(2,1)S(1)} %bitcast.217, f32[8192,512]{1,0:T(8,128)} %copy-done.1, f32[512]{0:T(512)S(1)} %broadcast_maximum_fusion, s32[512]{0:T(512)S(1)} %iota_add_fusion, s32[512]{0:T(512)S(1)} %dynamic_slice.10, s32[8192]{0:T(1024)} %param.19, bf16[1,128,2048]{2,1,0:T(8,128)(2,1)} %param.20, ...), kind=kOutput, calls=%fused_computation.26 | convolution fusion | flops 1376911360 | bytes 21536768 | tf_op jit(solution)/shard_map/dot_general | solution.py:81
  84.7 10.3 %all-to-all-start.2 = ((bf16[512,16,128]{2,0,1:T(8,128)(2,1)}), bf16[512,16,128]{2,0,1:T(8,128)(2,1)S(1)}, u32[]{:S(2)}, u32[]{:S(2)}) async-start(bf16[512,16,128]{2,0,1:T(8,128)(2,1)} %bitcast.213), calls=%async_computation.2 | async-start | bytes 4194304 | tf_op jit(solution)/shard_map/all_to_all | solution.py:20
  95.0 53.7 %all-to-all-done.2 = bf16[512,16,128]{2,0,1:T(8,128)(2,1)S(1)} async-done(((bf16[512,16,128]{2,0,1:T(8,128)(2,1)}), bf16[512,16,128]{2,0,1:T(8,128)(2,1)S(1)}, u32[]{:S(2)}, u32[]{:S(2)}) %all-to-all-start.2) | async-done | bytes 2097184 | tf_op jit(solution)/shard_map/all_to_all | solution.py:20
  156.1 9.3 %all-to-all-done.3 = f32[16,1,512]{2,1,0:T(1,128)S(1)} async-done(((f32[16,1,512]{2,1,0:T(1,128)}), f32[16,1,512]{2,1,0:T(1,128)S(1)}, u32[]{:S(2)}, u32[]{:S(2)}) %all-to-all-start.3) | async-done | bytes 32800 | tf_op jit(solution)/shard_map/all_to_all | solution.py:88
  173.7 18.3 %reduce-window.6 = s32[64,24,128]{2,1,0:T(8,128)S(1)} reduce-window(s32[64,24,128]{2,1,0:T(8,128)S(1)} %fusion.49, s32[]{:T(128)} %constant.42.clone.1), window={size=1x1x128 pad=0_0x0_0x127_0}, to_apply=%region_6.7 | reduce-window | flops 24969216 | bytes 1572868 | tf_op jit(solution)/shard_map/reduce-window
  193.6 11.8 %scatter_custom_fusion = s32[1024]{0:T(1024)S(1)} fusion(s32[3072]{0:T(1024)S(1)} %bitcast.228, s32[3072]{0:T(1024)S(1)} %add_select_fusion, s32[]{:T(128)} %constant.89.clone.1), kind=kCustom, calls=%fused_computation.86 | custom fusion | bytes 4100 | tf_op jit(solution)/shard_map/scatter | solution.py:129
  206.0 18.5 %all-to-all-done.4 = bf16[512,16,128]{2,0,1:T(8,128)(2,1)} async-done(((bf16[512,16,128]{2,0,1:T(8,128)(2,1)}), bf16[512,16,128]{2,0,1:T(8,128)(2,1)}, u32[]{:S(2)}, u32[]{:S(2)}) %all-to-all-start.4) | async-done | bytes 2097184 | tf_op jit(solution)/shard_map/all_to_all | solution.py:98
  226.4 6.0 %gather_fusion = bf16[1024,2048]{1,0:T(8,128)(2,1)} fusion(bf16[512,2048]{1,0:T(8,128)(2,1)S(1)} %copy_bitcast_fusion, s32[1024]{0:T(1024)S(1)} %maximum_clamp_fusion), kind=kCustom, calls=%fused_computation | custom fusion | bytes 8392704 | tf_op jit(solution)/shard_map/gather | solution.py:131
  235.0 50.8 %all_to_all.47 = bf16[16,1,64,2048]{3,2,1,0:T(8,128)(2,1)S(1)} all-to-all(bf16[16,1,64,2048]{3,2,1,0:T(8,128)(2,1)S(1)} %broadcast_select_fusion), channel_id=1, replica_groups=mesh['seq'=16,'hid'=16] {'seq'}, dimensions={0} | all-to-all | bytes 8388608 | tf_op jit(solution)/shard_map/all_to_all | solution.py:134
  291.3 8.0 %convert_bitcast_fusion = bf16[16,1,16,64,128]{4,3,0,2,1:T(8,128)(2,1)} fusion(bf16[352,2048]{1,0:T(8,128)(2,1)S(1)} %copy-done, bf16[16,1,64,2048]{3,2,1,0:T(8,128)(2,1)} %copy-done.2, f32[16,64,352]{2,1,0:T(8,128)} %fusion.9, bf16[352,2048]{1,0:T(8,128)(2,1)S(1)} %copy-done.10), kind=kOutput, calls=%fused_computation.17 | convolution fusion | flops 2957049856 | bytes 12713984 | tf_op jit(solution)/shard_map/sicf,ifnx->niscx/dot_general | solution.py:143
  299.2 5.5 %copy.76 = bf16[16,1,16,64,128]{4,3,2,0,1:T(8,128)(2,1)} copy(bf16[16,1,16,64,128]{4,3,0,2,1:T(8,128)(2,1)} %convert_bitcast_fusion) | data formatting | bytes 8388608 | tf_op jit(solution)/shard_map/convert_element_type | solution.py:145
  304.7 4.7 all-to-all-start.7
  318.1 79.5 %all-to-all-done.7 = bf16[16,1,1024,128]{3,2,1,0:T(8,128)(2,1)} async-done(((bf16[16,1,1024,128]{3,2,1,0:T(8,128)(2,1)}), bf16[16,1,1024,128]{3,2,1,0:T(8,128)(2,1)}, u32[]{:S(2)}, u32[]{:S(2)}) %all-to-all-start.7) | async-done | bytes 4194336 | tf_op jit(solution)/shard_map/all_to_all | solution.py:147
  397.6 12.5 %all-to-all-start.5 = ((bf16[512,16,128]{2,0,1:T(8,128)(2,1)}), bf16[512,16,128]{2,0,1:T(8,128)(2,1)S(1)}, u32[]{:S(2)}, u32[]{:S(2)}) async-start(bf16[512,16,128]{2,0,1:T(8,128)(2,1)} %bitcast.214), calls=%async_computation.5 | async-start | bytes 4194304 | tf_op jit(solution)/shard_map/all_to_all | solution.py:20
  414.0 36.1 %all-to-all-done.5 = bf16[512,16,128]{2,0,1:T(8,128)(2,1)S(1)} async-done(((bf16[512,16,128]{2,0,1:T(8,128)(2,1)}), bf16[512,16,128]{2,0,1:T(8,128)(2,1)S(1)}, u32[]{:S(2)}, u32[]{:S(2)}) %all-to-all-start.5) | async-done | bytes 2097184 | tf_op jit(solution)/shard_map/all_to_all | solution.py:20
  450.1 23.1 %all-to-all-start.8 = ((bf16[4,16,64,128]{3,2,0,1:T(8,128)(2,1)}), bf16[4,16,64,128]{3,2,0,1:T(8,128)(2,1)}, u32[]{:S(2)}, u32[]{:S(2)}) async-start(bf16[4,16,64,128]{3,2,0,1:T(8,128)(2,1)} %copy.78), calls=%async_computation.8 | async-start | bytes 2097152 | tf_op jit(solution)/shard_map/all_to_all | solution.py:155
  476.5 10.7 %all-to-all-done.8 = bf16[4,16,64,128]{3,2,0,1:T(8,128)(2,1)} async-done(((bf16[4,16,64,128]{3,2,0,1:T(8,128)(2,1)}), bf16[4,16,64,128]{3,2,0,1:T(8,128)(2,1)}, u32[]{:S(2)}, u32[]{:S(2)}) %all-to-all-start.8) | async-done | bytes 1048608 | tf_op jit(solution)/shard_map/all_to_all | solution.py:155
  488.5 9.2 %gather_fusion.1 = bf16[3072,128]{1,0:T(8,128)(2,1)S(1)} fusion(bf16[4096,128]{1,0:T(8,128)(2,1)S(1)} %bitcast.210, s32[3072]{0:T(1024)S(1)} %copy-done.6), kind=kCustom, calls=%fused_computation.1 | custom fusion | bytes 1585152 | tf_op jit(solution)/shard_map/gather | solution.py:163
  (70 shorter events, 56.0 us)
Async XLA Ops:
  0.0 291.3 %copy-start = (bf16[352,2048]{1,0:T(8,128)(2,1)S(1)}, bf16[352,2048]{1,0:T(8,128)(2,1)}, u32[]{:S(2)}) copy-start(bf16[352,2048]{1,0:T(8,128)(2,1)} %param.25) | copy-start | bytes 4325380
  0.0 32.6 %copy-start.5 = (bf16[512,1,128]{2,0,1:T(8,128)(2,1)S(1)}, bf16[512,1,128]{2,0,1:T(8,128)(2,1)}, u32[]{:S(2)}) copy-start(bf16[512,1,128]{2,0,1:T(8,128)(2,1)} %param.18) | copy-start | bytes 393220
  34.4 32.4 %all-to-all-start.1 = ((bf16[16,512,1,128]{3,1,2,0:T(8,128)(2,1)}), bf16[16,512,1,128]{3,1,2,0:T(8,128)(2,1)S(1)}, u32[]{:S(2)}, u32[]{:S(2)}) async-start(bf16[16,512,1,128]{3,1,2,0:T(8,128)(2,1)} %broadcast_in_dim.82), calls=%async_computation.1 | async-start | bytes 4194304 | tf_op jit(solution)/shard_map/all_to_all | solution.py:14
  41.4 12.8 %copy-start.7 = (s32[8192]{0:T(1024)S(1)}, s32[8192]{0:T(1024)}, u32[]{:S(2)}) copy-start(s32[8192]{0:T(1024)} %param.19) | copy-start | bytes 98308
  48.4 5.7 %copy-start.1 = (f32[8192,512]{1,0:T(8,128)}, f32[8192,512]{1,0:T(8,128)S(1)}, u32[]{:S(2)}) copy-start(f32[8192,512]{1,0:T(8,128)S(1)} %get-tuple-element.9) | copy-start | bytes 50331652
  84.7 64.0 %all-to-all-start.2 = ((bf16[512,16,128]{2,0,1:T(8,128)(2,1)}), bf16[512,16,128]{2,0,1:T(8,128)(2,1)S(1)}, u32[]{:S(2)}, u32[]{:S(2)}) async-start(bf16[512,16,128]{2,0,1:T(8,128)(2,1)} %bitcast.213), calls=%async_computation.2 | async-start | bytes 4194304 | tf_op jit(solution)/shard_map/all_to_all | solution.py:20
  148.9 0.7 copy-start.3
  149.6 23.3 %copy-start.8 = (s32[512,6]{0,1:T(8,128)S(1)}, s32[512,6]{0,1:T(8,128)}, u32[]{:S(2)}) copy-start(s32[512,6]{0,1:T(8,128)} %param.22) | copy-start | bytes 36868
  151.3 14.0 %all-to-all-start.3 = ((f32[16,1,512]{2,1,0:T(1,128)}), f32[16,1,512]{2,1,0:T(1,128)S(1)}, u32[]{:S(2)}, u32[]{:S(2)}) async-start(f32[16,1,512]{2,1,0:T(1,128)} %broadcast_in_dim.83), calls=%async_computation.3 | async-start | bytes 65536 | tf_op jit(solution)/shard_map/all_to_all | solution.py:88
  168.3 56.3 %all-to-all-start.4 = ((bf16[512,16,128]{2,0,1:T(8,128)(2,1)}), bf16[512,16,128]{2,0,1:T(8,128)(2,1)}, u32[]{:S(2)}, u32[]{:S(2)}) async-start(bf16[512,16,128]{2,0,1:T(8,128)(2,1)} %broadcast_in_dim.84), calls=%async_computation.4 | async-start | bytes 4194304 | tf_op jit(solution)/shard_map/all_to_all | solution.py:98
  235.0 52.8 %copy-start.9 = (bf16[352,2048]{1,0:T(8,128)(2,1)S(1)}, bf16[352,2048]{1,0:T(8,128)(2,1)}, u32[]{:S(2)}) copy-start(bf16[352,2048]{1,0:T(8,128)(2,1)} %param.24) | copy-start | bytes 4325380
  285.8 1.9 copy-start.2
  287.8 3.5 copy-start.10
  304.7 4.7 copy-start.11
  304.7 92.9 %all-to-all-start.7 = ((bf16[16,1,1024,128]{3,2,1,0:T(8,128)(2,1)}), bf16[16,1,1024,128]{3,2,1,0:T(8,128)(2,1)}, u32[]{:S(2)}, u32[]{:S(2)}) async-start(bf16[16,1,1024,128]{3,2,1,0:T(8,128)(2,1)} %bitcast.212), calls=%async_computation.7 | async-start | bytes 8388608 | tf_op jit(solution)/shard_map/all_to_all | solution.py:147
  397.6 52.5 %all-to-all-start.5 = ((bf16[512,16,128]{2,0,1:T(8,128)(2,1)}), bf16[512,16,128]{2,0,1:T(8,128)(2,1)S(1)}, u32[]{:S(2)}, u32[]{:S(2)}) async-start(bf16[512,16,128]{2,0,1:T(8,128)(2,1)} %bitcast.214), calls=%async_computation.5 | async-start | bytes 4194304 | tf_op jit(solution)/shard_map/all_to_all | solution.py:20
  450.1 37.1 %all-to-all-start.8 = ((bf16[4,16,64,128]{3,2,0,1:T(8,128)(2,1)}), bf16[4,16,64,128]{3,2,0,1:T(8,128)(2,1)}, u32[]{:S(2)}, u32[]{:S(2)}) async-start(bf16[4,16,64,128]{3,2,0,1:T(8,128)(2,1)} %copy.78), calls=%async_computation.8 | async-start | bytes 2097152 | tf_op jit(solution)/shard_map/all_to_all | solution.py:155
  475.5 13.0 %copy-start.6 = (s32[3072]{0:T(1024)S(1)}, s32[3072]{0:T(1024)}, u32[]{:S(2)}) copy-start(s32[3072]{0:T(1024)} %broadcast_clamp_fusion) | copy-start | bytes 36868
  488.5 11.1 %copy-start.4 = (f32[512,128]{1,0:T(8,128)S(1)}, f32[512,128]{1,0:T(8,128)}, u32[]{:S(2)}) copy-start(f32[512,128]{1,0:T(8,128)} %copy-done.3) | copy-start | bytes 786436

commit v2 on v1

--- a/solution.py
+++ b/solution.py
@@ -7,6 +7,7 @@
 FF = 1408
 TOP = 6
 CAP = 64
+LONGEST = 4096
 
 
 def seq_gather(rows, seq_count):
@@ -25,6 +26,17 @@
         tiled=True,
     )
     return jnp.sum(got.astype(jnp.float32), axis=1)
+
+
+def hid_permute_sum(part, hid_count, hid_index):
+    rows, width = part.shape
+    chunks = part.reshape(rows, hid_count, width // hid_count)
+    total = lax.dynamic_index_in_dim(chunks, hid_index, 1, keepdims=False).astype(jnp.float32)
+    for shift in range(1, hid_count):
+        sent = lax.dynamic_index_in_dim(chunks, (hid_index + shift) % hid_count, 1, keepdims=False)
+        pairs = [(i, (i + shift) % hid_count) for i in range(hid_count)]
+        total = total + lax.ppermute(sent, "hid", pairs).astype(jnp.float32)
+    return total
 
 
 def on_device(
@@ -56,14 +68,26 @@
     query_seg = lax.dynamic_slice_in_dim(segment_ids, query_first, tok_count)
     query_pos = query_first + jnp.arange(tok_count, dtype=jnp.int32)
     run_max = jnp.full((tok_count, local_heads), -1e30, jnp.float32)
-    key_part = seq_gather(key_rows, seq_count)
-    value_part = seq_gather(value_rows, seq_count)
+    window = min(seq_count, -(-LONGEST // tok_count) + 1)
+    both = jnp.concatenate([key_rows, value_rows], axis=1)
+    blocks = [both]
+    for shift in range(1, window):
+        pairs = [(i, i + shift) for i in range(seq_count - shift)]
+        blocks.append(lax.ppermute(both, "seq", pairs))
+    both_win = jnp.concatenate(blocks[::-1], axis=0)
+    key_part = both_win[:, :local_heads]
+    value_part = both_win[:, local_heads:]
     row_count = key_part.shape[0]
-    key_pos = jnp.arange(row_count, dtype=jnp.int32)
+    key_first = query_first - (window - 1) * tok_count
+    key_pos = key_first + jnp.arange(row_count, dtype=jnp.int32)
+    seg_padded = jnp.concatenate(
+        [jnp.full(((window - 1) * tok_count,), -1, jnp.int32), segment_ids]
+    )
+    key_seg = lax.dynamic_slice_in_dim(seg_padded, query_first, row_count)
     scores = (
         jnp.einsum("qhd,khd->qhk", queries, key_part, preferred_element_type=jnp.float32) * inv_root
     )
-    allowed = (query_seg[:, None] == segment_ids[None, :]) & (
+    allowed = (query_seg[:, None] == key_seg[None, :]) & (
         key_pos[None, :] <= query_pos[:, None]
     )
     scores = jnp.where(allowed[:, None, :], scores, -1e30)
@@ -84,24 +108,17 @@
     mixed_cols = lax.dynamic_slice_in_dim(stream, col_first, col_count, 1).astype(
         jnp.float32
     ) + hid_scatter_sum(partial_mix.astype(jnp.bfloat16), hid_count)
-    square_part = jnp.sum(mixed_cols * mixed_cols, axis=1)
-    square_all = lax.all_to_all(
-        jnp.broadcast_to(square_part[None, :], (hid_count, tok_count)),
-        "hid",
-        split_axis=0,
-        concat_axis=0,
-        tiled=True,
-    )
-    mean_square = (jnp.sum(square_all, axis=0) / width)[:, None]
-    gain_cols = lax.dynamic_slice_in_dim(norm_gain, col_first, col_count, 0)
-    normed_cols = (mixed_cols * lax.rsqrt(mean_square + 1e-06) * gain_cols).astype(jnp.bfloat16)
-    normed = lax.all_to_all(
-        jnp.broadcast_to(normed_cols[:, None, :], (tok_count, hid_count, col_count)),
+    mixed_all = lax.all_to_all(
+        jnp.broadcast_to(
+            mixed_cols.astype(jnp.bfloat16)[:, None, :], (tok_count, hid_count, col_count)
+        ),
         "hid",
         split_axis=1,
         concat_axis=1,
         tiled=True,
-    ).reshape(tok_count, width)
+    ).reshape(tok_count, width).astype(jnp.float32)
+    mean_square = jnp.mean(mixed_all * mixed_all, axis=1, keepdims=True)
+    normed = (mixed_all * lax.rsqrt(mean_square + 1e-06) * norm_gain).astype(jnp.bfloat16)
     shared_gate_val = jnp.einsum(
         "td,fd->tf", normed, shared_gate, preferred_element_type=jnp.float32
     )

time: 505 us -> 512 us (1.014)
  starting transfers between devices: 65.3 us -> 102 us
  blocking collectives: 82 us -> 50.8 us
  other arithmetic: 36.3 us -> 59.1 us
  waiting for transfers between devices: 214 us -> 196 us
  matrix products: 41.3 us -> 31.2 us
    all_to_all x3 -> x1, waiting for transfers between devices: 34.6 us -> 0.01 us  [on_device(): lax.all_to_all(jnp.broadcast_to(mixed_cols.astype(jnp.bfloat16)[:, None,...]
    all_to_all x1 -> x0, blocking collectives: 31.2 us -> none  [seq_gather(): got = lax.all_to_all(spread, 'seq', split_axis=0, concat_axis=0, tiled=True)]
    ppermute x0 -> x8, starting transfers between devices: none -> 24.1 us  [on_device(): blocks.append(lax.ppermute(both, 'seq', pairs))]
    ppermute x0 -> x8, waiting for transfers between devices: none -> 22.1 us  [on_device(): blocks.append(lax.ppermute(both, 'seq', pairs))]
    all_to_all x1, starting transfers between devices: 23.1 us -> 41.7 us  [on_device(): lax.all_to_all(expert_out.reshape(local_experts, seq_count, CAP, col_coun...]
    another operation x2, other arithmetic: 18.5 us -> 36.4 us
    all_to_all x3 -> x1, starting transfers between devices: 14.8 us -> 4.48 us  [on_device(): lax.all_to_all(jnp.broadcast_to(mixed_cols.astype(jnp.bfloat16)[:, None,...]
    dot_general x1, matrix products: 14.4 us -> 8.06 us  [on_device(): jnp.dot(attended, out_flat, preferred_element_type=jnp.float32)]
  transfers between devices with their start and end apart: 7 -> 13, of which waited for: 7 -> 8; matrix products, arithmetic and copies ran while one was open for 13% -> 17% of each run, Pallas kernels for 0% -> 0%
where the time goes in v2:
time: 512 us; the launch traced here: 505 us
  waiting for transfers between devices  196 us (38%)
  starting transfers between devices  102 us (20%)
  local copies, waits for them, and re-layouts  65.4 us (13%)
  other arithmetic  59.1 us (12%)
  blocking collectives  50.8 us (10%)
  matrix products  31.2 us (6%)
    all_to_all x2, waiting for transfers between devices, hid_scatter_sum(): lax.all_to_all(part.reshape(rows, hid_count, width // hid_count), 'hid',...  83.7 us
    all_to_all x1, waiting for transfers between devices, on_device(): lax.all_to_all(down_part, 'hid', split_axis=0, concat_axis=0, tiled=True)  79.3 us
    all_to_all x1, blocking collectives, on_device(): lax.all_to_all(send_rows, 'seq', split_axis=0, concat_axis=0, tiled=True)  50.8 us
    all_to_all x1, starting transfers between devices, on_device(): lax.all_to_all(expert_out.reshape(local_experts, seq_count, CAP, col_coun...  41.7 us
    another operation x2, other arithmetic  36.4 us
    ppermute x8, starting transfers between devices, on_device(): blocks.append(lax.ppermute(both, 'seq', pairs))  24.1 us
    all_to_all x2, starting transfers between devices, hid_scatter_sum(): lax.all_to_all(part.reshape(rows, hid_count, width // hid_count), 'hid',...  22.2 us
    ppermute x8, waiting for transfers between devices, on_device(): blocks.append(lax.ppermute(both, 'seq', pairs))  22.1 us
  transfers between devices with their start and end apart: 13, of which 8 were waited for; matrix products, arithmetic and copies ran while one was open for 17% of the time, Pallas kernels for 0%

profile of v2, /device:TPU:2, one launch (start us, length us, event | category | flops | bytes accessed | tf_op | source)
XLA Modules:
  0.0 505.0 jit_solution(17655521724245121680)
XLA Ops:
  16.1 7.9 %collective-permute-done = bf16[512,2,128]{2,0,1:T(8,128)(2,1)S(1)} collective-permute-done((bf16[512,2,128]{2,0,1:T(8,128)(2,1)S(1)}, bf16[512,2,128]{2,0,1:T(8,128)(2,1)S(1)}, u32[]{:S(2)}, u32[]{:S(2)}) %collective-permute-start) | collective-permute-done | bytes 262176 | tf_op jit(solution)/shard_map/ppermute | solution.py:76
  25.9 4.2 collective-permute-start.6
  30.2 5.5 %collective-permute-start.7 = (bf16[512,2,128]{2,0,1:T(8,128)(2,1)S(1)}, bf16[512,2,128]{2,0,1:T(8,128)(2,1)S(1)}, u32[]{:S(2)}, u32[]{:S(2)}) collective-permute-start(bf16[512,2,128]{2,0,1:T(8,128)(2,1)S(1)} %constant_dynamic-update-slice_fusion), channel_id=1, source_target_pairs={{0,16},{16,32},{32,48},{48,64},{64,80},{80,96},{96,112},{112,128},... | collective-permute-start | bytes 786440 | tf_op jit(solution)/shard_map/ppermute | solution.py:76
  35.8 7.5 %collective-permute-done.3 = bf16[512,2,128]{2,0,1:T(8,128)(2,1)S(1)} collective-permute-done((bf16[512,2,128]{2,0,1:T(8,128)(2,1)S(1)}, bf16[512,2,128]{2,0,1:T(8,128)(2,1)S(1)}, u32[]{:S(2)}, u32[]{:S(2)}) %collective-permute-start.3) | collective-permute-done | bytes 262176 | tf_op jit(solution)/shard_map/ppermute | solution.py:76
  43.3 5.6 %collective-permute-done.4 = bf16[512,2,128]{2,0,1:T(8,128)(2,1)S(1)} collective-permute-done((bf16[512,2,128]{2,0,1:T(8,128)(2,1)S(1)}, bf16[512,2,128]{2,0,1:T(8,128)(2,1)S(1)}, u32[]{:S(2)}, u32[]{:S(2)}) %collective-permute-start.4) | collective-permute-done | bytes 262176 | tf_op jit(solution)/shard_map/ppermute | solution.py:76
  56.1 4.1 fusion.1
  60.2 8.1 %fusion.13 = bf16[64,16,8,128]{3,2,1,0:T(8,128)(2,1)S(1)} fusion(f32[4608,512]{1,0:T(8,128)} %copy-done.2, f32[512]{0:T(512)S(1)} %broadcast_maximum_fusion, s32[512]{0:T(512)S(1)} %iota_add_fusion.1, s32[512]{0:T(512)S(1)} %dynamic_slice.10, s32[4608]{0:T(1024)} %copy-done.11, s32[4608]{0:T(1024)} %copy-done.10, bf16[4608,2,128]{2,0,1:T(8,128)(2,1)} %copy-done.14, ...), kind=kOutput, calls=%fused_computation.30 | convolution fusion | flops 892469248 | bytes 13287424 | tf_op jit(solution)/shard_map/dot_general | solution.py:105
  70.2 11.2 %all-to-all-start = ((bf16[512,16,128]{2,0,1:T(8,128)(2,1)}), bf16[512,16,128]{2,0,1:T(8,128)(2,1)S(1)}, u32[]{:S(2)}, u32[]{:S(2)}) async-start(bf16[512,16,128]{2,0,1:T(8,128)(2,1)} %bitcast.219), calls=%async_computation | async-start | bytes 4194304 | tf_op jit(solution)/shard_map/all_to_all | solution.py:21
  81.4 48.7 %all-to-all-done = bf16[512,16,128]{2,0,1:T(8,128)(2,1)S(1)} async-done(((bf16[512,16,128]{2,0,1:T(8,128)(2,1)}), bf16[512,16,128]{2,0,1:T(8,128)(2,1)S(1)}, u32[]{:S(2)}, u32[]{:S(2)}) %all-to-all-start) | async-done | bytes 2097184 | tf_op jit(solution)/shard_map/all_to_all | solution.py:21
  133.8 4.5 all-to-all-start.1
  145.3 34.8 %reduce-window.6 = s32[64,24,128]{2,1,0:T(8,128)} reduce-window(s32[64,24,128]{2,1,0:T(8,128)} %fusion.50, s32[]{:T(128)} %constant.41.clone.1), window={size=1x1x128 pad=0_0x0_0x127_0}, to_apply=%region_5.6 | reduce-window | flops 24969216 | bytes 1572868 | tf_op jit(solution)/shard_map/reduce-window
  189.9 12.1 %scatter_custom_fusion = s32[1024]{0:T(1024)S(1)} fusion(s32[3072]{0:T(1024)S(1)} %bitcast.230, s32[3072]{0:T(1024)} %add_select_fusion, s32[]{:T(128)} %constant.86.clone.1), kind=kCustom, calls=%fused_computation.105 | custom fusion | bytes 4608 | tf_op jit(solution)/shard_map/scatter | solution.py:146
  205.6 6.0 %gather_fusion = bf16[1024,2048]{1,0:T(8,128)(2,1)} fusion(bf16[512,2048]{1,0:T(8,128)(2,1)S(1)} %fusion.8, s32[1024]{0:T(1024)S(1)} %maximum_clamp_fusion), kind=kCustom, calls=%fused_computation | custom fusion | bytes 8392704 | tf_op jit(solution)/shard_map/gather | solution.py:148
  214.2 50.8 %all_to_all.30 = bf16[16,1,64,2048]{3,2,1,0:T(8,128)(2,1)S(1)} all-to-all(bf16[16,1,64,2048]{3,2,1,0:T(8,128)(2,1)S(1)} %broadcast_select_fusion), channel_id=1, replica_groups=mesh['seq'=16,'hid'=16] {'seq'}, dimensions={0} | all-to-all | bytes 8388608 | tf_op jit(solution)/shard_map/all_to_all | solution.py:151
  270.5 8.4 %convert_bitcast_fusion.1 = bf16[16,1,16,64,128]{4,3,0,2,1:T(8,128)(2,1)} fusion(bf16[352,2048]{1,0:T(8,128)(2,1)S(1)} %copy-done, bf16[16,1,64,2048]{3,2,1,0:T(8,128)(2,1)} %copy-done.3, f32[16,64,352]{2,1,0:T(8,128)} %fusion.11, bf16[352,2048]{1,0:T(8,128)(2,1)} %param.26), kind=kOutput, calls=%fused_computation.22 | convolution fusion | flops 2957049856 | bytes 12713984 | tf_op jit(solution)/shard_map/sicf,ifnx->niscx/dot_general | solution.py:160
  278.9 5.5 %copy.47 = bf16[16,1,16,64,128]{4,3,2,0,1:T(8,128)(2,1)} copy(bf16[16,1,16,64,128]{4,3,0,2,1:T(8,128)(2,1)} %convert_bitcast_fusion.1) | data formatting | bytes 8388608 | tf_op jit(solution)/shard_map/convert_element_type | solution.py:162
  284.4 9.7 %all-to-all-start.4 = ((bf16[16,1,1024,128]{3,2,1,0:T(8,128)(2,1)}), bf16[16,1,1024,128]{3,2,1,0:T(8,128)(2,1)}, u32[]{:S(2)}, u32[]{:S(2)}) async-start(bf16[16,1,1024,128]{3,2,1,0:T(8,128)(2,1)} %bitcast.218), calls=%async_computation.4 | async-start | bytes 8388608 | tf_op jit(solution)/shard_map/all_to_all | solution.py:164
  296.8 4.4 fusion.14
  304.7 79.3 %all-to-all-done.4 = bf16[16,1,1024,128]{3,2,1,0:T(8,128)(2,1)} async-done(((bf16[16,1,1024,128]{3,2,1,0:T(8,128)(2,1)}), bf16[16,1,1024,128]{3,2,1,0:T(8,128)(2,1)}, u32[]{:S(2)}, u32[]{:S(2)}) %all-to-all-start.4) | async-done | bytes 4194336 | tf_op jit(solution)/shard_map/all_to_all | solution.py:164
  384.0 11.0 %all-to-all-start.2 = ((bf16[512,16,128]{2,0,1:T(8,128)(2,1)}), bf16[512,16,128]{2,0,1:T(8,128)(2,1)S(1)}, u32[]{:S(2)}, u32[]{:S(2)}) async-start(bf16[512,16,128]{2,0,1:T(8,128)(2,1)} %bitcast.220), calls=%async_computation.2 | async-start | bytes 4194304 | tf_op jit(solution)/shard_map/all_to_all | solution.py:21
  398.9 35.0 %all-to-all-done.2 = bf16[512,16,128]{2,0,1:T(8,128)(2,1)S(1)} async-done(((bf16[512,16,128]{2,0,1:T(8,128)(2,1)}), bf16[512,16,128]{2,0,1:T(8,128)(2,1)S(1)}, u32[]{:S(2)}, u32[]{:S(2)}) %all-to-all-start.2) | async-done | bytes 2097184 | tf_op jit(solution)/shard_map/all_to_all | solution.py:21
  434.0 41.7 %all-to-all-start.5 = ((bf16[4,16,64,128]{3,2,0,1:T(8,128)(2,1)}), bf16[4,16,64,128]{3,2,0,1:T(8,128)(2,1)}, u32[]{:S(2)}, u32[]{:S(2)}) async-start(bf16[4,16,64,128]{3,2,0,1:T(8,128)(2,1)} %copy.49), calls=%async_computation.5 | async-start | bytes 2097152 | tf_op jit(solution)/shard_map/all_to_all | solution.py:172
  479.0 10.7 %all-to-all-done.5 = bf16[4,16,64,128]{3,2,0,1:T(8,128)(2,1)} async-done(((bf16[4,16,64,128]{3,2,0,1:T(8,128)(2,1)}), bf16[4,16,64,128]{3,2,0,1:T(8,128)(2,1)}, u32[]{:S(2)}, u32[]{:S(2)}) %all-to-all-start.5) | async-done | bytes 1048608 | tf_op jit(solution)/shard_map/all_to_all | solution.py:172
  491.0 9.2 %gather_fusion.1 = bf16[3072,128]{1,0:T(8,128)(2,1)S(1)} fusion(bf16[4096,128]{1,0:T(8,128)(2,1)S(1)} %bitcast.216, s32[3072]{0:T(1024)S(1)} %copy-done.13), kind=kCustom, calls=%fused_computation.1 | custom fusion | bytes 1585152 | tf_op jit(solution)/shard_map/gather | solution.py:180
  (101 shorter events, 78.6 us)
Async XLA Ops:
  0.0 270.5 %copy-start = (bf16[352,2048]{1,0:T(8,128)(2,1)S(1)}, bf16[352,2048]{1,0:T(8,128)(2,1)}, u32[]{:S(2)}) copy-start(bf16[352,2048]{1,0:T(8,128)(2,1)} %param.25) | copy-start | bytes 4325380
  0.0 50.2 %copy-start.7 = (bf16[512,1,128]{2,0,1:T(8,128)(2,1)S(1)}, bf16[512,1,128]{2,0,1:T(8,128)(2,1)}, u32[]{:S(2)}) copy-start(bf16[512,1,128]{2,0,1:T(8,128)(2,1)} %param.17) | copy-start | bytes 393220
  1.0 49.2 %copy-start.8 = (bf16[512,1,128]{2,0,1:T(8,128)(2,1)S(1)}, bf16[512,1,128]{2,0,1:T(8,128)(2,1)}, u32[]{:S(2)}) copy-start(bf16[512,1,128]{2,0,1:T(8,128)(2,1)} %param.18) | copy-start | bytes 393220
  2.0 21.9 %collective-permute-start = (bf16[512,2,128]{2,0,1:T(8,128)(2,1)S(1)}, bf16[512,2,128]{2,0,1:T(8,128)(2,1)S(1)}, u32[]{:S(2)}, u32[]{:S(2)}) collective-permute-start(bf16[512,2,128]{2,0,1:T(8,128)(2,1)S(1)} %constant_dynamic-update-slice_fusion), channel_id=1, source_target_pairs={{0,128},{16,144},{32,160},{48,176},{64,192},{80,208},{96,224},{112... | collective-permute-start | bytes 786440 | tf_op jit(solution)/shard_map/ppermute | solution.py:76
  6.1 19.8 %collective-permute-start.1 = (bf16[512,2,128]{2,0,1:T(8,128)(2,1)S(1)}, bf16[512,2,128]{2,0,1:T(8,128)(2,1)S(1)}, u32[]{:S(2)}, u32[]{:S(2)}) collective-permute-start(bf16[512,2,128]{2,0,1:T(8,128)(2,1)S(1)} %constant_dynamic-update-slice_fusion), channel_id=1, source_target_pairs={{0,112},{16,128},{32,144},{48,160},{64,176},{80,192},{96,208},{112... | collective-permute-start | bytes 786440 | tf_op jit(solution)/shard_map/ppermute | solution.py:76
  7.6 22.7 %collective-permute-start.2 = (bf16[512,2,128]{2,0,1:T(8,128)(2,1)S(1)}, bf16[512,2,128]{2,0,1:T(8,128)(2,1)S(1)}, u32[]{:S(2)}, u32[]{:S(2)}) collective-permute-start(bf16[512,2,128]{2,0,1:T(8,128)(2,1)S(1)} %constant_dynamic-update-slice_fusion), channel_id=1, source_target_pairs={{0,96},{16,112},{32,128},{48,144},{64,160},{80,176},{96,192},{112,... | collective-permute-start | bytes 786440 | tf_op jit(solution)/shard_map/ppermute | solution.py:76
  9.4 33.9 %collective-permute-start.3 = (bf16[512,2,128]{2,0,1:T(8,128)(2,1)S(1)}, bf16[512,2,128]{2,0,1:T(8,128)(2,1)S(1)}, u32[]{:S(2)}, u32[]{:S(2)}) collective-permute-start(bf16[512,2,128]{2,0,1:T(8,128)(2,1)S(1)} %constant_dynamic-update-slice_fusion), channel_id=1, source_target_pairs={{0,80},{16,96},{32,112},{48,128},{64,144},{80,160},{96,176},{112,1... | collective-permute-start | bytes 786440 | tf_op jit(solution)/shard_map/ppermute | solution.py:76
  11.7 37.2 %collective-permute-start.4 = (bf16[512,2,128]{2,0,1:T(8,128)(2,1)S(1)}, bf16[512,2,128]{2,0,1:T(8,128)(2,1)S(1)}, u32[]{:S(2)}, u32[]{:S(2)}) collective-permute-start(bf16[512,2,128]{2,0,1:T(8,128)(2,1)S(1)} %constant_dynamic-update-slice_fusion), channel_id=1, source_target_pairs={{0,64},{16,80},{32,96},{48,112},{64,128},{80,144},{96,160},{112,17... | collective-permute-start | bytes 786440 | tf_op jit(solution)/shard_map/ppermute | solution.py:76
  15.3 37.2 %copy-start.10 = (s32[4608]{0:T(1024)}, s32[4608]{0:T(1024)S(1)}, u32[]{:S(2)}) copy-start(s32[4608]{0:T(1024)S(1)} %get-tuple-element.10) | copy-start | bytes 55300
  15.3 37.2 %copy-start.11 = (s32[4608]{0:T(1024)}, s32[4608]{0:T(1024)S(1)}, u32[]{:S(2)}) copy-start(s32[4608]{0:T(1024)S(1)} %get-tuple-element.11) | copy-start | bytes 55300
  16.1 34.2 %copy-start.17 = (bf16[512,1,128]{2,0,1:T(8,128)(2,1)S(1)}, bf16[512,1,128]{2,0,1:T(8,128)(2,1)}, u32[]{:S(2)}) copy-start(bf16[512,1,128]{2,0,1:T(8,128)(2,1)} %param.16) | copy-start | bytes 393220
  24.0 26.1 %collective-permute-start.5 = (bf16[512,2,128]{2,0,1:T(8,128)(2,1)S(1)}, bf16[512,2,128]{2,0,1:T(8,128)(2,1)S(1)}, u32[]{:S(2)}, u32[]{:S(2)}) collective-permute-start(bf16[512,2,128]{2,0,1:T(8,128)(2,1)S(1)} %constant_dynamic-update-slice_fusion), channel_id=1, source_target_pairs={{0,48},{16,64},{32,80},{48,96},{64,112},{80,128},{96,144},{112,160... | collective-permute-start | bytes 786440 | tf_op jit(solution)/shard_map/ppermute | solution.py:76
  25.9 24.2 %collective-permute-start.6 = (bf16[512,2,128]{2,0,1:T(8,128)(2,1)S(1)}, bf16[512,2,128]{2,0,1:T(8,128)(2,1)S(1)}, u32[]{:S(2)}, u32[]{:S(2)}) collective-permute-start(bf16[512,2,128]{2,0,1:T(8,128)(2,1)S(1)} %constant_dynamic-update-slice_fusion), channel_id=1, source_target_pairs={{0,32},{16,48},{32,64},{48,80},{64,96},{80,112},{96,128},{112,144}... | collective-permute-start | bytes 786440 | tf_op jit(solution)/shard_map/ppermute | solution.py:76
  30.2 20.0 %collective-permute-start.7 = (bf16[512,2,128]{2,0,1:T(8,128)(2,1)S(1)}, bf16[512,2,128]{2,0,1:T(8,128)(2,1)S(1)}, u32[]{:S(2)}, u32[]{:S(2)}) collective-permute-start(bf16[512,2,128]{2,0,1:T(8,128)(2,1)S(1)} %constant_dynamic-update-slice_fusion), channel_id=1, source_target_pairs={{0,16},{16,32},{32,48},{48,64},{64,80},{80,96},{96,112},{112,128},... | collective-permute-start | bytes 786440 | tf_op jit(solution)/shard_map/ppermute | solution.py:76
  70.2 59.9 %all-to-all-start = ((bf16[512,16,128]{2,0,1:T(8,128)(2,1)}), bf16[512,16,128]{2,0,1:T(8,128)(2,1)S(1)}, u32[]{:S(2)}, u32[]{:S(2)}) async-start(bf16[512,16,128]{2,0,1:T(8,128)(2,1)} %bitcast.219), calls=%async_computation | async-start | bytes 4194304 | tf_op jit(solution)/shard_map/all_to_all | solution.py:21
  133.8 4.5 copy-start.15
  133.8 68.4 %all-to-all-start.1 = ((bf16[512,16,128]{2,0,1:T(8,128)(2,1)}), bf16[512,16,128]{2,0,1:T(8,128)(2,1)S(1)}, u32[]{:S(2)}, u32[]{:S(2)}) async-start(bf16[512,16,128]{2,0,1:T(8,128)(2,1)} %broadcast_in_dim.58), calls=%async_computation.1 | async-start | bytes 4194304 | tf_op jit(solution)/shard_map/all_to_all | solution.py:111
  214.2 52.8 %copy-start.16 = (bf16[352,2048]{1,0:T(8,128)(2,1)S(1)}, bf16[352,2048]{1,0:T(8,128)(2,1)}, u32[]{:S(2)}) copy-start(bf16[352,2048]{1,0:T(8,128)(2,1)} %param.24) | copy-start | bytes 4325380
  284.4 99.6 %all-to-all-start.4 = ((bf16[16,1,1024,128]{3,2,1,0:T(8,128)(2,1)}), bf16[16,1,1024,128]{3,2,1,0:T(8,128)(2,1)}, u32[]{:S(2)}, u32[]{:S(2)}) async-start(bf16[16,1,1024,128]{3,2,1,0:T(8,128)(2,1)} %bitcast.218), calls=%async_computation.4 | async-start | bytes 8388608 | tf_op jit(solution)/shard_map/all_to_all | solution.py:164
  384.0 50.0 %all-to-all-start.2 = ((bf16[512,16,128]{2,0,1:T(8,128)(2,1)}), bf16[512,16,128]{2,0,1:T(8,128)(2,1)S(1)}, u32[]{:S(2)}, u32[]{:S(2)}) async-start(bf16[512,16,128]{2,0,1:T(8,128)(2,1)} %bitcast.220), calls=%async_computation.2 | async-start | bytes 4194304 | tf_op jit(solution)/shard_map/all_to_all | solution.py:21
  397.9 79.6 %copy-start.12 = (s32[3072,1]{0,1:T(1,128)S(1)}, s32[3072,1]{0,1:T(1,128)}, u32[]{:S(2)}) copy-start(s32[3072,1]{0,1:T(1,128)} %get-tuple-element.5) | copy-start | bytes 36868
  434.0 55.7 %all-to-all-start.5 = ((bf16[4,16,64,128]{3,2,0,1:T(8,128)(2,1)}), bf16[4,16,64,128]{3,2,0,1:T(8,128)(2,1)}, u32[]{:S(2)}, u32[]{:S(2)}) async-start(bf16[4,16,64,128]{3,2,0,1:T(8,128)(2,1)} %copy.49), calls=%async_computation.5 | async-start | bytes 2097152 | tf_op jit(solution)/shard_map/all_to_all | solution.py:172
  478.0 13.0 %copy-start.13 = (s32[3072]{0:T(1024)S(1)}, s32[3072]{0:T(1024)}, u32[]{:S(2)}) copy-start(s32[3072]{0:T(1024)} %broadcast_clamp_fusion) | copy-start | bytes 36868
  491.0 10.4 %copy-start.9 = (bf16[512,6,1]{1,2,0:T(2,128)(2,1)S(1)}, bf16[512,6,1]{1,2,0:T(2,128)(2,1)}, u32[]{:S(2)}) copy-start(bf16[512,6,1]{1,2,0:T(2,128)(2,1)} %copy.52) | copy-start | bytes 18436
  (7 other events, 16.1 us)
